TPU v7x, 32 devices: a whole 2x2x4 slice. The times are simulated.
32 devices in a mesh: dp: 4 (over z), ctx: 8 (over y, x, core).
Axes of the slice: x: 2, y: 2, z: 4, core: 2. Of those that a mesh axis runs over, the one named last changes fastest.
Arguments:
- tokens: bfloat16 [4, 1024, 6144], P('dp', 'ctx'), may hold values from -0.1875 to 0.1875
- cotangent: bfloat16 [4, 1024, 6144], P('dp', 'ctx'), may hold values from -6 to 6
- w_router: float32 [6144], replicated, may hold values from -2 to 2
- w_query: bfloat16 [6144, 4096], P(None, 'ctx'), may hold values from -0.078125 to 0.078125
- w_key: bfloat16 [6144, 4096], P(None, 'ctx'), may hold values from -0.078125 to 0.078125
- w_value: bfloat16 [6144, 4096], P(None, 'ctx'), may hold values from -0.078125 to 0.078125
- w_out: bfloat16 [4096, 6144], P('ctx'), may hold values from -0.09375 to 0.09375
- chosen: int32 [4, 160], P('dp', 'ctx'), may hold values from -1 to 1023, as said below
- counts: int32 [4, 8], P('dp', 'ctx'), may hold values from 12 to 20, as said below
Outputs:
- layer_out: bfloat16 [4, 1024, 6144], P('dp', 'ctx')
- grad_query: bfloat16 [6144, 4096], P('dp', 'ctx')
- grad_key: bfloat16 [6144, 4096], P('dp', 'ctx')
- grad_value: bfloat16 [6144, 4096], P('dp', 'ctx')
- grad_out: bfloat16 [4096, 6144], P('ctx', 'dp')
- grad_router: float32 [6144], replicated
Inputs may be any that keep to these rules, and one draw needn't show every extreme that they name: `chosen`: for every sequence b and device block c, the first counts[b, c] of the block's slots c * 20 to (c + 1) * 20 - 1 hold increasing positions of that device's tokens, c * 128 to (c + 1) * 128 - 1; the other slots hold -1. In every sequence the counts add up to 128, and some device's block has exactly 20 used slots.
All inputs are finite; a program needn't handle non-finite values.
Results may differ from a plain program's by a relative error of at most 0.018.
Values may be sent and summed in bfloat16 or wider, within the bound.
No kernel may reach another device: no remote copies, remote signals or barrier semaphores. Data moves between devices by JAX's collectives and lax.ppermute only.
A program may use at most 128 MiB of HBM per device.

v0:
```python
import math
import jax
import jax.numpy as jnp
from jax import lax
from jax.sharding import PartitionSpec as P

HDIM = 128
HIGHEST_PRECISION = lax.Precision.HIGHEST


def head_norm(values, width):
    shaped = values.reshape(values.shape[0], -1, width)
    inverse = lax.rsqrt(jnp.mean(shaped * shaped, axis=-1, keepdims=True) + 1e-06)
    return (shaped * inverse, inverse)


def norm_back(grad_hat, normal, inverse):
    return inverse * (grad_hat - normal * jnp.mean(grad_hat * normal, axis=-1, keepdims=True))


def rounded_term(part):
    return lax.optimization_barrier(part.astype(jnp.bfloat16)).astype(jnp.float32)


def body(n_dp, n_ctx, tokens, cotangent, w_router, w_query, w_key, w_value, w_out, chosen, counts):
    length = tokens.shape[1]
    width = tokens.shape[2]
    capacity = chosen.shape[1]
    inner = w_query.shape[1]
    heads_here = inner // HDIM
    scale = 1.0 / math.sqrt(HDIM)
    offset = lax.axis_index("ctx") * length
    slot_ids = lax.broadcasted_iota(jnp.int32, (capacity,), 0)
    local = chosen[0] - offset
    present = (slot_ids < counts[0, 0]) & (local >= 0) & (local < length)
    columns = lax.broadcasted_iota(jnp.int32, (capacity, length), 1)
    onehot = ((local[:, None] == columns) & present[:, None]).astype(jnp.bfloat16)
    rows = jnp.dot(onehot, tokens[0], preferred_element_type=jnp.float32)
    rows_back = jnp.dot(onehot, cotangent[0], preferred_element_type=jnp.float32)
    logits = jnp.dot(rows, w_router, precision=HIGHEST_PRECISION)
    weights = jax.nn.sigmoid(logits)
    normed = (rows * lax.rsqrt(jnp.mean(rows * rows, axis=-1, keepdims=True) + 1e-05)).astype(
        jnp.bfloat16
    )
    delta = (weights[:, None] * rows_back).astype(jnp.bfloat16)
    flag_cols = jnp.zeros((capacity, HDIM), jnp.bfloat16).at[:, 0].set(present.astype(jnp.bfloat16))
    packed = lax.all_gather(
        jnp.concatenate([normed, delta, flag_cols], axis=1), "ctx", axis=0, tiled=False
    )
    chunk_normed = packed[:, :, :width]
    chunk_delta = packed[:, :, width : 2 * width]
    all_present = packed[:, :, 2 * width].reshape(n_ctx * capacity)
    slots = n_ctx * capacity
    block = width // n_dp
    own_blocks = lax.all_to_all(jnp.concatenate([normed, delta], axis=0), "dp", 1, 0, tiled=True)
    pieces = lax.all_gather(own_blocks, "ctx", axis=0, tiled=False).reshape(
        n_ctx, n_dp, 2, capacity, block
    )
    normed_blocks = pieces[:, :, 0].transpose(1, 0, 2, 3).reshape(n_dp * slots, block)
    delta_blocks = pieces[:, :, 1].transpose(1, 0, 2, 3).reshape(n_dp * slots, block)

    def project(weight):
        raw = lax.dot_general(
            chunk_normed, weight, (((2,), (0,)), ((), ())), preferred_element_type=jnp.float32
        )
        return raw.reshape(slots, inner)

    query_raw = project(w_query)
    key_raw = project(w_key)
    value_raw = project(w_value)
    query_hat, query_scale = head_norm(query_raw, HDIM)
    key_hat, key_scale = head_norm(key_raw, HDIM)
    query_b = query_hat.astype(jnp.bfloat16)
    key_b = key_hat.astype(jnp.bfloat16)
    value_b = value_raw.reshape(slots, heads_here, HDIM).astype(jnp.bfloat16)
    current = lax.broadcasted_iota(jnp.int32, (slots, slots), 0)
    earlier = lax.broadcasted_iota(jnp.int32, (slots, slots), 1)
    allowed = (earlier <= current) & ((all_present[None, :] > 0.5) | (earlier == current))
    scores = jnp.einsum("ihd,jhd->hij", query_b, key_b, preferred_element_type=jnp.float32) * scale
    exponent = jnp.where(allowed[None], jnp.exp(scores), 0.0)
    attend = exponent / jnp.sum(exponent, axis=-1, keepdims=True)
    attend_b = attend.astype(jnp.bfloat16)
    mixed = jnp.einsum("hij,jhd->ihd", attend_b, value_b, preferred_element_type=jnp.float32)
    mixed = mixed.astype(jnp.bfloat16).reshape(slots, inner)
    mixed_back = lax.dot_general(
        chunk_delta, w_out, (((2,), (1,)), ((), ())), preferred_element_type=jnp.float32
    )
    mixed_back = mixed_back.astype(jnp.bfloat16).reshape(slots, heads_here, HDIM)
    attend_back = jnp.einsum(
        "ihd,jhd->hij", mixed_back, value_b, preferred_element_type=jnp.float32
    )
    inner_sum = jnp.sum(attend * attend_back, axis=-1, keepdims=True)
    scores_back = (attend * (attend_back - inner_sum) * scale).astype(jnp.bfloat16)
    value_back = jnp.einsum(
        "hij,ihd->jhd", attend_b, mixed_back, preferred_element_type=jnp.float32
    )
    value_back = value_back.astype(jnp.bfloat16).reshape(slots, inner)
    qhat_back = jnp.einsum("hij,jhd->ihd", scores_back, key_b, preferred_element_type=jnp.float32)
    khat_back = jnp.einsum("hij,ihd->jhd", scores_back, query_b, preferred_element_type=jnp.float32)
    query_back = (
        norm_back(qhat_back, query_hat, query_scale).astype(jnp.bfloat16).reshape(slots, inner)
    )
    key_back = norm_back(khat_back, key_hat, key_scale).astype(jnp.bfloat16).reshape(slots, inner)
    mixed_late, query_back, key_back, value_back = lax.optimization_barrier(
        (mixed, query_back, key_back, value_back)
    )
    contributions = lax.dot_general(
        mixed_late.reshape(n_ctx, capacity, inner),
        w_out,
        (((2,), (0,)), ((), ())),
        preferred_element_type=jnp.float32,
    ).astype(jnp.bfloat16)
    received = lax.all_to_all(contributions, "ctx", 0, 0, tiled=True)
    update = jnp.sum(received.astype(jnp.float32), axis=0)
    scaled = weights[:, None] * update
    spread = jnp.dot(onehot.astype(jnp.float32).T, scaled, precision=HIGHEST_PRECISION)
    layer_out = (tokens[0].astype(jnp.float32) + spread).astype(jnp.bfloat16)[None]
    gate_back = jnp.sum(rows_back * update, axis=-1) * weights * (1.0 - weights)
    router_part = jnp.dot(gate_back, rows, precision=HIGHEST_PRECISION)
    router_group = jnp.sum(lax.all_gather(router_part, "ctx", axis=0, tiled=False), axis=0)
    factors = lax.all_gather(
        jnp.concatenate([query_back, key_back, value_back], axis=1), "dp", axis=0, tiled=False
    ).reshape(n_dp * slots, 3 * inner)

    def contract(left, right):
        return lax.dot_general(
            left, right, (((0,), (0,)), ((), ())), preferred_element_type=jnp.float32
        ).astype(jnp.bfloat16)

    grads = contract(normed_blocks, factors)
    grad_query = grads[:, :inner]
    grad_key = grads[:, inner : 2 * inner]
    grad_value = grads[:, 2 * inner :]
    dp_index = lax.axis_index("dp")
    delta_by_seq = delta_blocks.reshape(n_dp, slots, block)
    out_total = lax.dot_general(
        mixed,
        lax.dynamic_index_in_dim(delta_by_seq, dp_index, 0, keepdims=False),
        (((0,), (0,)), ((), ())),
        preferred_element_type=jnp.float32,
    )
    for shift in range(1, n_dp):
        arrived = lax.ppermute(mixed, "dp", [(i, (i + shift) % n_dp) for i in range(n_dp)])
        source = (dp_index + n_dp - shift) % n_dp
        out_total = out_total + lax.dot_general(
            arrived,
            lax.dynamic_index_in_dim(delta_by_seq, source, 0, keepdims=False),
            (((0,), (0,)), ((), ())),
            preferred_element_type=jnp.float32,
        )
    grad_out = out_total.astype(jnp.bfloat16)
    router_pieces = lax.dynamic_update_index_in_dim(
        jnp.zeros((n_dp,) + router_group.shape, jnp.float32), router_group, dp_index, 0
    )
    for shift in range(1, n_dp):
        arrived = lax.ppermute(router_group, "dp", [(i, (i + shift) % n_dp) for i in range(n_dp)])
        router_pieces = lax.dynamic_update_index_in_dim(
            router_pieces, arrived, (dp_index + n_dp - shift) % n_dp, 0
        )
    grad_router = jnp.sum(router_pieces, axis=0)
    return (layer_out, grad_query, grad_key, grad_value, grad_out, grad_router)


def solution(mesh):
    n_dp = mesh.shape["dp"]
    n_ctx = mesh.shape["ctx"]
    in_specs = (
        P("dp", "ctx", None),
        P("dp", "ctx", None),
        P(),
        P(None, "ctx"),
        P(None, "ctx"),
        P(None, "ctx"),
        P("ctx", None),
        P("dp", "ctx"),
        P("dp", "ctx"),
    )
    out_specs = (
        P("dp", "ctx", None),
        P("dp", "ctx"),
        P("dp", "ctx"),
        P("dp", "ctx"),
        P("ctx", "dp"),
        P(),
    )

    def run(*args):
        return body(n_dp, n_ctx, *args)

    return jax.shard_map(run, mesh=mesh, in_specs=in_specs, out_specs=out_specs, check_vma=False)
```

profile of v0, /device:TPU:0, one launch (start us, length us, event | category | flops | bytes accessed | tf_op | source)
XLA Modules:
  0.0 164.5 jit_solution(2579473443318761461)
XLA Ops:
  9.2 1.9 %multiply_reduce_fusion.2 = (f32[20]{0:T(128)S(1)}, f32[20,6144]{1,0:T(8,128)S(1)}) fusion(bf16[1,128,6144]{2,1,0:T(8,128)(2,1)} %param.11, s32[20]{0:T(128)S(1)} %bitcast.142, pred[20]{0:T(512)(128)(4,1)S(1)} %get-tuple-element.26), kind=kOutput, calls=%fused_computation.61 | convolution fusion | flops 31708140 | bytes 2064564 | tf_op jit(solution)/shard_map/dot_general | solution.py:38
  11.1 1.4 fusion.44
  12.9 1.2 multiply_convert_fusion
  14.8 0.9 fusion.50
  15.8 20.0 %all_to_all.21 = bf16[40,4,1536]{2,0,1:T(8,128)(2,1)} all-to-all(bf16[40,4,1536]{2,0,1:T(8,128)(2,1)S(1)} %bitcast.130), channel_id=1, replica_groups=mesh['dp'=4,'ctx'=8] {'dp'}, dimensions={1} | all-to-all | bytes 983040 | tf_op jit(solution)/shard_map/all_to_all | solution.py:55
  35.9 21.7 %all-gather.12.cloned.1.call-done = bf16[8,20,12416]{2,1,0:T(8,128)(2,1)} async-done(((bf16[1,20,12416]{2,1,0:T(8,128)(2,1)}), bf16[8,20,12416]{2,1,0:T(8,128)(2,1)}) %all-gather.12.cloned.1.call-update) | async-done | bytes 3973136 | tf_op jit(solution)/shard_map/all_gather | solution.py:47
  57.6 4.9 %fusion.8 = f32[8,20,512]{2,1,0:T(8,128)S(1)} fusion(bf16[6144,512]{1,0:T(8,128)(2,1)} %param.14, bf16[8,20,12416]{2,1,0:T(8,128)(2,1)} %all-gather.12.cloned.1.call-done), kind=kOutput, calls=%fused_computation.11 | convolution fusion | flops 1006632960 | bytes 8978432 | tf_op jit(solution)/shard_map/dot_general | solution.py:63
  63.0 5.0 %fusion.6 = f32[8,20,512]{2,1,0:T(8,128)S(1)} fusion(bf16[6144,512]{1,0:T(8,128)(2,1)} %param.15, bf16[8,20,12416]{2,1,0:T(8,128)(2,1)} %all-gather.12.cloned.1.call-done), kind=kOutput, calls=%fused_computation.9 | convolution fusion | flops 1006632960 | bytes 8978432 | tf_op jit(solution)/shard_map/dot_general | solution.py:63
  68.4 1.0 compare_reduce_fusion
  69.6 4.9 %fusion.29 = bf16[8,20,512]{2,1,0:T(8,128)(2,1)S(1)} fusion(bf16[6144,512]{1,0:T(8,128)(2,1)} %param.16, bf16[8,20,12416]{2,1,0:T(8,128)(2,1)} %all-gather.12.cloned.1.call-done), kind=kOutput, calls=%fused_computation.41 | convolution fusion | flops 1006714880 | bytes 8814592 | tf_op jit(solution)/shard_map/dot_general | solution.py:63
  75.5 1.5 collective-permute-start
  76.9 2.4 %collective-permute-start.2 = (bf16[160,512]{1,0:T(8,128)(2,1)S(1)}, bf16[160,512]{1,0:T(8,128)(2,1)}, u32[]{:S(2)}, u32[]{:S(2)}) collective-permute-start(bf16[160,512]{1,0:T(8,128)(2,1)S(1)} %bitcast.132), channel_id=1, source_target_pairs={{0,24},{8,0},{16,8},{24,16},{1,25},{9,1},{17,9},{25,17},{2,26},{10... | collective-permute-start | bytes 491528 | tf_op jit(solution)/shard_map/ppermute | solution.py:143
  79.9 6.3 %fusion.34 = bf16[8,20,512]{2,1,0:T(8,128)(2,1)S(1)} fusion(bf16[512,6144]{1,0:T(8,128)(2,1)} %param.17, bf16[8,20,12416]{2,1,0:T(8,128)(2,1)} %all-gather.12.cloned.1.call-done), kind=kOutput, calls=%fused_computation.42 | convolution fusion | flops 1006714880 | bytes 8814592 | tf_op jit(solution)/shard_map/dot_general | solution.py:85
  88.6 5.7 %convolution_convert_fusion.1 = bf16[8,20,6144]{2,1,0:T(8,128)(2,1)} fusion(bf16[8,20,512]{2,1,0:T(8,128)(2,1)S(1)} %reshape.193, bf16[512,6144]{1,0:T(8,128)(2,1)} %param.17), kind=kOutput, calls=%fused_computation.2 | convolution fusion | flops 1007616000 | bytes 8421376 | tf_op jit(solution)/shard_map/dot_general | solution.py:107
  94.3 4.4 %all-to-all-start = ((bf16[8,20,6144]{2,1,0:T(8,128)(2,1)}), bf16[8,20,6144]{2,1,0:T(8,128)(2,1)}, u32[]{:S(2)}, u32[]{:S(2)}) async-start(bf16[8,20,6144]{2,1,0:T(8,128)(2,1)} %convolution_convert_fusion.1), calls=%async_computation | async-start | bytes 4718592 | tf_op jit(solution)/shard_map/all_to_all | solution.py:113
  99.8 4.3 %copy.144 = bf16[8,160,1536]{2,0,1:T(8,128)(2,1)S(1)} copy(bf16[8,160,1536]{2,1,0:T(8,128)(2,1)} %all-gather.8.cloned.1.call-done) | data formatting | bytes 7864320 | tf_op jit(solution)/shard_map/all_gather | solution.py:56
  104.3 1.5 copy.146
  105.8 5.0 %constant_dynamic-slice_fusion.1 = (bf16[1,160,1536]{2,0,1:T(2,128)(2,1)}, bf16[1,160,1536]{2,0,1:T(2,128)(2,1)}, bf16[1,160,1536]{2,0,1:T(2,128)(2,1)S(1)}, bf16[1,160,1536]{2,0,1:T(2,128)(2,1)S(1)}) fusion(bf16[4,160,1536]{2,0,1:T(4,128)(2,1)S(1)} %bitcast.126, s32[]{:T(128)S(6)} %select_n.48, s32[]{:T(128)S(6)} %select_n.50, s32[]{:T(128)S(6)} %select_n.46, ...), kind=kLoop, calls=%fused_computation.130 | loop fusion | bytes 3932176 | tf_op jit(solution)/shard_map/jit(dynamic_index_in_dim)/dynamic_slice | solution.py:147
  112.2 1.5 convolution_add_fusion.2
  113.7 2.0 %copy.145 = bf16[4,8,20,1536]{3,2,1,0:T(8,128)(2,1)} copy(bf16[4,8,20,1536]{3,1,2,0:T(8,128)(2,1)S(1)} %get-tuple-element.32) | data formatting | bytes 3932160 | tf_op jit(solution)/shard_map/transpose | solution.py:59
  115.7 4.0 %reshape.195 = bf16[640,1536]{1,0:T(8,128)(2,1)} reshape(bf16[4,8,20,1536]{3,2,1,0:T(8,128)(2,1)} %copy.145) | data formatting | bytes 3932160 | tf_op jit(solution)/shard_map/reshape | solution.py:59
  119.7 2.0 %fusion.52 = f32[512,1536]{1,0:T(8,128)S(1)} fusion(bf16[160,512]{1,0:T(8,128)(2,1)} %collective-permute-done.2, bf16[1,160,1536]{2,0,1:T(2,128)(2,1)} %get-tuple-element.34), kind=kOutput, calls=%fused_computation.65 | convolution fusion | flops 251658240 | bytes 3801088 | tf_op jit(solution)/shard_map/dot_general | solution.py:145
  121.7 1.8 %fusion.13 = bf16[512,1536]{1,0:T(8,128)(2,1)} fusion(f32[512,1536]{1,0:T(8,128)S(1)} %fusion.52, f32[512,1536]{1,0:T(8,128)S(1)} %convolution_add_fusion.2, bf16[160,512]{1,0:T(8,128)(2,1)S(1)} %collective-permute-done.1, bf16[1,160,1536]{2,0,1:T(2,128)(2,1)S(1)} %copy-done.6), kind=kOutput, calls=%fused_computation.19 | convolution fusion | flops 254017536 | bytes 8519680 | tf_op jit(solution)/shard_map/dot_general | solution.py:145
  123.5 4.6 %all-to-all-done = bf16[8,20,6144]{2,1,0:T(8,128)(2,1)} async-done(((bf16[8,20,6144]{2,1,0:T(8,128)(2,1)}), bf16[8,20,6144]{2,1,0:T(8,128)(2,1)}, u32[]{:S(2)}, u32[]{:S(2)}) %all-to-all-start) | async-done | bytes 1966112 | tf_op jit(solution)/shard_map/all_to_all | solution.py:113
  128.1 2.1 %convert_reduce_fusion = f32[20,6144]{1,0:T(8,128)S(1)} fusion(bf16[8,20,6144]{2,1,0:T(8,128)(2,1)} %all-to-all-done), kind=kLoop, calls=%fused_computation.15 | loop fusion | flops 1843200 | bytes 2457600 | tf_op jit(solution)/shard_map/reduce_sum | solution.py:114
  130.8 8.3 %all-gather.2 = f32[49152]{0:T(1024)S(1)} all-gather(f32[6144]{0:T(1024)S(1)} %bitcast.136), channel_id=4, replica_groups=mesh['dp'=4,'ctx'=8] {'ctx'}, dimensions={0}, use_global_device_ids=true | all-gather | bytes 221184 | tf_op jit(solution)/shard_map/all_gather | solution.py:120
  139.2 1.5 collective-permute-start.3
  140.8 1.0 collective-permute-start.4
  141.7 2.8 %collective-permute-start.5 = (f32[6144]{0:T(1024)S(1)}, f32[6144]{0:T(1024)S(1)}, u32[]{:S(2)}, u32[]{:S(2)}) collective-permute-start(f32[6144]{0:T(1024)S(1)} %reduce_sum.108), channel_id=1, source_target_pairs={{0,24},{8,0},{16,8},{24,16},{1,25},{9,1},{17,9},{25,17},{2,26},{10... | collective-permute-start | bytes 73736 | tf_op jit(solution)/shard_map/ppermute | solution.py:156
  144.6 2.8 %fusion.2 = bf16[1,128,6144]{2,1,0:T(8,128)(2,1)} fusion(bf16[1,128,6144]{2,1,0:T(8,128)(2,1)S(1)} %copy-done.4, f32[20,6144]{1,0:T(8,128)S(1)} %convert_reduce_fusion, f32[20]{0:T(128)S(1)} %fusion.44, s32[20]{0:T(128)S(1)} %bitcast.144, pred[20]{0:T(512)(128)(4,1)S(1)} %get-tuple-element.26), kind=kOutput, calls=%fused_computation.5 | convolution fusion | flops 191230976 | bytes 3637428 | tf_op jit(solution)/shard_map/dot_general | solution.py:116
  149.6 6.1 %convolution_convert_fusion = bf16[1536,1536]{1,0:T(8,128)(2,1)S(1)} fusion(bf16[640,1536]{1,0:T(8,128)(2,1)} %reshape.195, bf16[640,1536]{1,0:T(8,128)(2,1)} %all-gather.10.cloned.1.call-done), kind=kOutput, calls=%fused_computation.1 | convolution fusion | flops 3022258176 | bytes 8650752 | tf_op jit(solution)/shard_map/dot_general | solution.py:126
  155.7 2.3 %fusion.109 = (bf16[1536,512]{1,0:T(8,128)(2,1)}, bf16[1536,512]{1,0:T(8,128)(2,1)}, bf16[1536,512]{1,0:T(8,128)(2,1)}) fusion(bf16[1536,1536]{1,0:T(8,128)(2,1)S(1)} %convolution_convert_fusion), kind=kLoop, calls=%fused_computation.146 | loop fusion | bytes 9437184 | tf_op jit(solution)/shard_map/slice | solution.py:133
  (78 shorter events, 12.8 us)
Async XLA Ops:
  7.2 5.8 %copy-start = (bf16[1,128,6144]{2,1,0:T(8,128)(2,1)S(1)}, bf16[1,128,6144]{2,1,0:T(8,128)(2,1)}, u32[]{:S(2)}) copy-start(bf16[1,128,6144]{2,1,0:T(8,128)(2,1)} %param.12) | copy-start | bytes 4718596
  7.2 50.4 %all-gather.12.cloned.1.call-start = ((), (), s32[]{:S(2)}) async-start(), calls=%async_computation.4 | async-start | bytes 5363712 | tf_op jit(solution)/shard_map/all_gather | solution.py:47
  11.1 1.5 copy-start.2
  15.7 84.1 %all-gather.8.cloned.1.call-start = ((), (), s32[]{:S(2)}) async-start(), calls=%async_computation.2 | async-start | bytes 4423680 | tf_op jit(solution)/shard_map/all_gather | solution.py:56
  75.5 36.0 %collective-permute-start = (bf16[160,512]{1,0:T(8,128)(2,1)S(1)}, bf16[160,512]{1,0:T(8,128)(2,1)S(1)}, u32[]{:S(2)}, u32[]{:S(2)}) collective-permute-start(bf16[160,512]{1,0:T(8,128)(2,1)S(1)} %bitcast.131), channel_id=1, source_target_pairs={{0,8},{8,16},{16,24},{24,0},{1,9},{9,17},{17,25},{25,1},{2,10},{10... | collective-permute-start | bytes 491528 | tf_op jit(solution)/shard_map/ppermute | solution.py:143
  76.9 42.8 %collective-permute-start.2 = (bf16[160,512]{1,0:T(8,128)(2,1)S(1)}, bf16[160,512]{1,0:T(8,128)(2,1)}, u32[]{:S(2)}, u32[]{:S(2)}) collective-permute-start(bf16[160,512]{1,0:T(8,128)(2,1)S(1)} %bitcast.132), channel_id=1, source_target_pairs={{0,24},{8,0},{16,8},{24,16},{1,25},{9,1},{17,9},{25,17},{2,26},{10... | collective-permute-start | bytes 491528 | tf_op jit(solution)/shard_map/ppermute | solution.py:143
  79.3 42.4 %collective-permute-start.1 = (bf16[160,512]{1,0:T(8,128)(2,1)S(1)}, bf16[160,512]{1,0:T(8,128)(2,1)S(1)}, u32[]{:S(2)}, u32[]{:S(2)}) collective-permute-start(bf16[160,512]{1,0:T(8,128)(2,1)S(1)} %bitcast.133), channel_id=1, source_target_pairs={{0,16},{8,24},{16,0},{24,8},{1,17},{9,25},{17,1},{25,9},{2,18},{10... | collective-permute-start | bytes 491528 | tf_op jit(solution)/shard_map/ppermute | solution.py:143
  94.3 33.8 %all-to-all-start = ((bf16[8,20,6144]{2,1,0:T(8,128)(2,1)}), bf16[8,20,6144]{2,1,0:T(8,128)(2,1)}, u32[]{:S(2)}, u32[]{:S(2)}) async-start(bf16[8,20,6144]{2,1,0:T(8,128)(2,1)} %convolution_convert_fusion.1), calls=%async_computation | async-start | bytes 4718592 | tf_op jit(solution)/shard_map/all_to_all | solution.py:113
  98.7 50.9 %all-gather.10.cloned.1.call-start = ((), (), s32[]{:S(2)}) async-start(), calls=%async_computation.3 | async-start | bytes 2457600 | tf_op jit(solution)/shard_map/all_gather | solution.py:121
  111.5 0.7 copy-start.7
  119.7 2.0 %copy-start.6 = (bf16[1,160,1536]{2,0,1:T(2,128)(2,1)S(1)}, bf16[1,160,1536]{2,0,1:T(2,128)(2,1)}, u32[]{:S(2)}) copy-start(bf16[1,160,1536]{2,0,1:T(2,128)(2,1)} %get-tuple-element.33) | copy-start | bytes 1474564
  123.5 6.7 %copy-start.5 = (f32[20,6144]{1,0:T(8,128)S(1)}, f32[20,6144]{1,0:T(8,128)}, u32[]{:S(2)}) copy-start(f32[20,6144]{1,0:T(8,128)} %get-tuple-element.40) | copy-start | bytes 1474564
  123.5 6.9 %copy-start.3 = (f32[20,6144]{1,0:T(8,128)S(1)}, f32[20,6144]{1,0:T(8,128)}, u32[]{:S(2)}) copy-start(f32[20,6144]{1,0:T(8,128)} %copy-done.2) | copy-start | bytes 1474564
  123.5 21.1 %copy-start.4 = (bf16[1,128,6144]{2,1,0:T(8,128)(2,1)S(1)}, bf16[1,128,6144]{2,1,0:T(8,128)(2,1)}, u32[]{:S(2)}) copy-start(bf16[1,128,6144]{2,1,0:T(8,128)(2,1)} %param.11) | copy-start | bytes 4718596
  139.2 8.5 %collective-permute-start.3 = (f32[6144]{0:T(1024)S(1)}, f32[6144]{0:T(1024)S(1)}, u32[]{:S(2)}, u32[]{:S(2)}) collective-permute-start(f32[6144]{0:T(1024)S(1)} %reduce_sum.108), channel_id=1, source_target_pairs={{0,8},{8,16},{16,24},{24,0},{1,9},{9,17},{17,25},{25,1},{2,10},{10... | collective-permute-start | bytes 73736 | tf_op jit(solution)/shard_map/ppermute | solution.py:156
  140.8 7.4 %collective-permute-start.4 = (f32[6144]{0:T(1024)S(1)}, f32[6144]{0:T(1024)S(1)}, u32[]{:S(2)}, u32[]{:S(2)}) collective-permute-start(f32[6144]{0:T(1024)S(1)} %reduce_sum.108), channel_id=1, source_target_pairs={{0,16},{8,24},{16,0},{24,8},{1,17},{9,25},{17,1},{25,9},{2,18},{10... | collective-permute-start | bytes 73736 | tf_op jit(solution)/shard_map/ppermute | solution.py:156
  141.7 6.8 %collective-permute-start.5 = (f32[6144]{0:T(1024)S(1)}, f32[6144]{0:T(1024)S(1)}, u32[]{:S(2)}, u32[]{:S(2)}) collective-permute-start(f32[6144]{0:T(1024)S(1)} %reduce_sum.108), channel_id=1, source_target_pairs={{0,24},{8,0},{16,8},{24,16},{1,25},{9,1},{17,9},{25,17},{2,26},{10... | collective-permute-start | bytes 73736 | tf_op jit(solution)/shard_map/ppermute | solution.py:156
  149.6 8.4 %copy-start.1 = (bf16[1,128,6144]{2,1,0:T(8,128)(2,1)S(1)}, bf16[1,128,6144]{2,1,0:T(8,128)(2,1)}, u32[]{:S(2)}) copy-start(bf16[1,128,6144]{2,1,0:T(8,128)(2,1)} %param.12) | copy-start | bytes 4718596
Sparse Core Ops, SparseCore 0:
  15.8 41.8 all-gather.11
  59.5 35.6 all-gather.7
  101.1 45.1 all-gather.9
where the time goes:
time: 165 us
  matrix products  49 us (30%)
  blocking collectives  28.3 us (17%)
  waiting for transfers between devices  26.4 us (16%)
  local copies, waits for them, and re-layouts  22.6 us (14%)
  between operations  14.8 us (9%)
  starting transfers between devices  14.4 us (9%)
  other arithmetic  8.98 us (5%)
    all_gather x1, waiting for transfers between devices, body(): lax.all_gather(jnp.concatenate([normed, delta, flag_cols], axis=1), 'ctx'...  21.7 us
    all_to_all x1, blocking collectives, body(): lax.all_to_all(jnp.concatenate([normed, delta], axis=0), 'dp', 1, 0, tile...  20 us
    dot_general x3, matrix products, project(): lax.dot_general(chunk_normed, weight, (((2,), (0,)), ((), ())), preferred...  14.8 us
    all_gather x1, blocking collectives, body(): lax.all_gather(router_part, 'ctx', axis=0, tiled=False)  8.3 us
    dot_general x1, matrix products, body(): lax.dot_general(chunk_delta, w_out, (((2,), (1,)), ((), ())), preferred_e...  6.33 us
    dot_general x1, matrix products, contract(): lax.dot_general(left, right, (((0,), (0,)), ((), ())), preferred_element_...  6.13 us
    dot_general x1, matrix products, body(): lax.dot_general(mixed_late.reshape(n_ctx, capacity, inner), w_out, (((2,)...  5.71 us
    ppermute x3, starting transfers between devices, body(): lax.ppermute(router_group, 'dp', [(i, (i + shift) % n_dp) for i in range(...  5.36 us
  transfers between devices with their start and end apart: 10, of which 2 were waited for; matrix products, arithmetic and copies ran while one was open for 39% of the time, Pallas kernels for 0%

commit v1 on v0

--- a/solution.py
+++ b/solution.py
@@ -52,7 +52,16 @@
     all_present = packed[:, :, 2 * width].reshape(n_ctx * capacity)
     slots = n_ctx * capacity
     block = width // n_dp
-    own_blocks = lax.all_to_all(jnp.concatenate([normed, delta], axis=0), "dp", 1, 0, tiled=True)
+    shard = jnp.concatenate([normed, delta], axis=0)
+    ways, here = (lax.axis_size("dp"), lax.axis_index("dp"))
+    width_2 = shard.shape[1] // ways
+    turned = jnp.roll(shard, -here * width_2, axis=1)
+    got = [lax.slice_in_dim(turned, 0, width_2, axis=1)]
+    for far in range(1, ways):
+        sent = lax.slice_in_dim(turned, far * width_2, (far + 1) * width_2, axis=1)
+        got.append(lax.ppermute(sent, "dp", [(d, (d + far) % ways) for d in range(ways)]))
+    line = jnp.concatenate(got[::-1], axis=0)
+    own_blocks = jnp.roll(line, (here + 1) * got[0].shape[0], axis=0)
     pieces = lax.all_gather(own_blocks, "ctx", axis=0, tiled=False).reshape(
         n_ctx, n_dp, 2, capacity, block
     )

time: 165 us -> 168 us (1.018)
  blocking collectives: 28.3 us -> 8.43 us
  waiting for transfers between devices: 26.4 us -> 36.4 us
  local copies, waits for them, and re-layouts: 22.6 us -> 28.8 us
  starting transfers between devices: 14.4 us -> 18.8 us
  other arithmetic: 8.98 us -> 10.7 us
    all_to_all x1 -> x0, blocking collectives: 20 us -> none  [body(): lax.all_to_all(jnp.concatenate([normed, delta], axis=0), 'dp', 1, 0, tile...]
    ppermute x0 -> x3, waiting for transfers between devices: none -> 9.93 us  [body(): lax.ppermute(sent, 'dp', [(d, (d + far) % ways) for d in range(ways)])]
    reshape x0 -> x1, local copies, waits for them, and re-layouts: none -> 6.82 us  [body(): lax.all_gather(own_blocks, 'ctx', axis=0, tiled=False)]
    ppermute x0 -> x3, starting transfers between devices: none -> 6.11 us  [body(): lax.ppermute(sent, 'dp', [(d, (d + far) % ways) for d in range(ways)])]
    all_gather x1 -> x0, local copies, waits for them, and re-layouts: 4.27 us -> none  [body(): lax.all_gather(own_blocks, 'ctx', axis=0, tiled=False)]
    ppermute x3, starting transfers between devices: 5.36 us -> 2.08 us  [body(): lax.ppermute(router_group, 'dp', [(i, (i + shift) % n_dp) for i in range(...]
    all_to_all x1, waiting for transfers between devices: 4.57 us -> 1.47 us  [body(): received = lax.all_to_all(contributions, 'ctx', 0, 0, tiled=True)]
    transpose x2, local copies, waits for them, and re-layouts: 1.77 us -> 4.16 us  [body(): pieces[:, :, 1].transpose(1, 0, 2, 3).reshape(n_dp * slots, block)]
  transfers between devices with their start and end apart: 10 -> 13, of which waited for: 2 -> 5; matrix products, arithmetic and copies ran while one was open for 39% -> 43% of each run, Pallas kernels for 0% -> 0%
where the time goes in v1:
time: 168 us; the launch traced here: 167 us
  matrix products  48.9 us (29%)
  waiting for transfers between devices  36.4 us (22%)
  local copies, waits for them, and re-layouts  28.8 us (17%)
  starting transfers between devices  18.8 us (11%)
  between operations  14.9 us (9%)
  other arithmetic  10.7 us (6%)
  blocking collectives  8.43 us (5%)
    all_gather x1, waiting for transfers between devices, body(): lax.all_gather(jnp.concatenate([normed, delta, flag_cols], axis=1), 'ctx'...  22.9 us
    dot_general x3, matrix products, project(): lax.dot_general(chunk_normed, weight, (((2,), (0,)), ((), ())), preferred...  14.9 us
    ppermute x3, waiting for transfers between devices, body(): lax.ppermute(sent, 'dp', [(d, (d + far) % ways) for d in range(ways)])  9.93 us
    all_gather x1, blocking collectives, body(): lax.all_gather(router_part, 'ctx', axis=0, tiled=False)  8.43 us
    reshape x1, local copies, waits for them, and re-layouts, body(): lax.all_gather(own_blocks, 'ctx', axis=0, tiled=False)  6.82 us
    ppermute x3, starting transfers between devices, body(): lax.ppermute(mixed, 'dp', [(i, (i + shift) % n_dp) for i in range(n_dp)])  6.15 us
    dot_general x1, matrix products, contract(): lax.dot_general(left, right, (((0,), (0,)), ((), ())), preferred_element_...  6.13 us
    ppermute x3, starting transfers between devices, body(): lax.ppermute(sent, 'dp', [(d, (d + far) % ways) for d in range(ways)])  6.11 us
  transfers between devices with their start and end apart: 13, of which 5 were waited for; matrix products, arithmetic and copies ran while one was open for 43% of the time, Pallas kernels for 0%

profile of v1, /device:TPU:0, one launch (start us, length us, event | category | flops | bytes accessed | tf_op | source)
XLA Modules:
  0.0 167.0 jit_solution(426771288786683549)
XLA Ops:
  9.4 1.9 %multiply_reduce_fusion.2 = (f32[20]{0:T(128)S(1)}, f32[20,6144]{1,0:T(8,128)S(1)}) fusion(bf16[1,128,6144]{2,1,0:T(8,128)(2,1)} %param.11, s32[20]{0:T(128)S(1)} %bitcast.126, pred[20]{0:T(512)(128)(4,1)S(1)} %get-tuple-element.26), kind=kOutput, calls=%fused_computation.65 | convolution fusion | flops 31708140 | bytes 2064564 | tf_op jit(solution)/shard_map/dot_general | solution.py:38
  11.3 1.4 fusion.44
  12.9 1.2 multiply_convert_fusion
  15.7 1.8 %fusion.53 = bf16[40,6144]{1,0:T(8,128)(2,1)S(1)} fusion(s32[]{:T(128)S(6)} %select_n.67, bf16[20,6144]{1,0:T(8,128)(2,1)S(1)} %multiply_convert_fusion.1, bf16[20,6144]{1,0:T(8,128)(2,1)S(1)} %get-tuple-element.42), kind=kLoop, calls=%fused_computation.67 | loop fusion | flops 1966080 | bytes 983044 | tf_op jit(solution)/shard_map/jit(_roll_dynamic)/concatenate | solution.py:58
  17.6 5.1 %collective-permute-start = (bf16[40,1536]{1,0:T(8,128)(2,1)S(1)}, bf16[40,1536]{1,0:T(8,128)(2,1)S(1)}, u32[]{:S(2)}, u32[]{:S(2)}) collective-permute-start(bf16[40,1536]{1,0:T(8,128)(2,1)S(1)} %get-tuple-element.39), channel_id=1, source_target_pairs={{0,24},{8,0},{16,8},{24,16},{1,25},{9,1},{17,9},{25,17},{2,26},{10... | collective-permute-start | bytes 368648 | tf_op jit(solution)/shard_map/ppermute | solution.py:62
  23.7 2.7 %collective-permute-done = bf16[40,1536]{1,0:T(8,128)(2,1)S(1)} collective-permute-done((bf16[40,1536]{1,0:T(8,128)(2,1)S(1)}, bf16[40,1536]{1,0:T(8,128)(2,1)S(1)}, u32[]{:S(2)}, u32[]{:S(2)}) %collective-permute-start) | collective-permute-done | bytes 122912 | tf_op jit(solution)/shard_map/ppermute | solution.py:62
  26.5 7.2 %collective-permute-done.1 = bf16[40,1536]{1,0:T(8,128)(2,1)S(1)} collective-permute-done((bf16[40,1536]{1,0:T(8,128)(2,1)S(1)}, bf16[40,1536]{1,0:T(8,128)(2,1)S(1)}, u32[]{:S(2)}, u32[]{:S(2)}) %collective-permute-start.1) | collective-permute-done | bytes 122912 | tf_op jit(solution)/shard_map/ppermute | solution.py:62
  34.8 22.9 %all-gather.13.cloned.1.call-done = bf16[8,20,12416]{2,1,0:T(8,128)(2,1)} async-done(((bf16[1,20,12416]{2,1,0:T(8,128)(2,1)}), bf16[8,20,12416]{2,1,0:T(8,128)(2,1)}) %all-gather.13.cloned.1.call-update) | async-done | bytes 3973136 | tf_op jit(solution)/shard_map/all_gather | solution.py:47
  58.7 4.9 %fusion.29 = bf16[8,20,512]{2,1,0:T(8,128)(2,1)S(1)} fusion(bf16[6144,512]{1,0:T(8,128)(2,1)} %param.16, bf16[8,20,12416]{2,1,0:T(8,128)(2,1)} %all-gather.13.cloned.1.call-done), kind=kOutput, calls=%fused_computation.41 | convolution fusion | flops 1006714880 | bytes 8814592 | tf_op jit(solution)/shard_map/dot_general | solution.py:72
  63.7 5.0 %fusion.6 = f32[8,20,512]{2,1,0:T(8,128)S(1)} fusion(bf16[6144,512]{1,0:T(8,128)(2,1)} %param.15, bf16[8,20,12416]{2,1,0:T(8,128)(2,1)} %all-gather.13.cloned.1.call-done), kind=kOutput, calls=%fused_computation.9 | convolution fusion | flops 1006632960 | bytes 8978432 | tf_op jit(solution)/shard_map/dot_general | solution.py:72
  68.9 4.9 %fusion.8 = f32[8,20,512]{2,1,0:T(8,128)S(1)} fusion(bf16[6144,512]{1,0:T(8,128)(2,1)} %param.14, bf16[8,20,12416]{2,1,0:T(8,128)(2,1)} %all-gather.13.cloned.1.call-done), kind=kOutput, calls=%fused_computation.11 | convolution fusion | flops 1006632960 | bytes 8978432 | tf_op jit(solution)/shard_map/dot_general | solution.py:72
  76.8 2.3 %collective-permute-start.4 = (bf16[160,512]{1,0:T(8,128)(2,1)}, bf16[160,512]{1,0:T(8,128)(2,1)}, u32[]{:S(2)}, u32[]{:S(2)}) collective-permute-start(bf16[160,512]{1,0:T(8,128)(2,1)} %bitcast.115), channel_id=1, source_target_pairs={{0,16},{8,24},{16,0},{24,8},{1,17},{9,25},{17,1},{25,9},{2,18},{10... | collective-permute-start | bytes 491528 | tf_op jit(solution)/shard_map/ppermute | solution.py:152
  79.2 1.5 collective-permute-start.3
  80.6 2.3 %collective-permute-start.5 = (bf16[160,512]{1,0:T(8,128)(2,1)}, bf16[160,512]{1,0:T(8,128)(2,1)}, u32[]{:S(2)}, u32[]{:S(2)}) collective-permute-start(bf16[160,512]{1,0:T(8,128)(2,1)} %bitcast.115), channel_id=1, source_target_pairs={{0,24},{8,0},{16,8},{24,16},{1,25},{9,1},{17,9},{25,17},{2,26},{10... | collective-permute-start | bytes 491528 | tf_op jit(solution)/shard_map/ppermute | solution.py:152
  83.0 5.7 %fusion.34 = bf16[8,20,512]{2,1,0:T(8,128)(2,1)S(1)} fusion(bf16[512,6144]{1,0:T(8,128)(2,1)} %param.17, bf16[8,20,12416]{2,1,0:T(8,128)(2,1)} %all-gather.13.cloned.1.call-done), kind=kOutput, calls=%fused_computation.42 | convolution fusion | flops 1006714880 | bytes 8814592 | tf_op jit(solution)/shard_map/dot_general | solution.py:94
  92.0 5.7 %convolution_convert_fusion.1 = bf16[8,20,6144]{2,1,0:T(8,128)(2,1)} fusion(bf16[8,20,512]{2,1,0:T(8,128)(2,1)S(1)} %reshape.189, bf16[512,6144]{1,0:T(8,128)(2,1)} %param.17), kind=kOutput, calls=%fused_computation.2 | convolution fusion | flops 1007616000 | bytes 8421376 | tf_op jit(solution)/shard_map/dot_general | solution.py:116
  97.7 4.4 %all-to-all-start = ((bf16[8,20,6144]{2,1,0:T(8,128)(2,1)}), bf16[8,20,6144]{2,1,0:T(8,128)(2,1)}, u32[]{:S(2)}, u32[]{:S(2)}) async-start(bf16[8,20,6144]{2,1,0:T(8,128)(2,1)} %convolution_convert_fusion.1), calls=%async_computation | async-start | bytes 4718592 | tf_op jit(solution)/shard_map/all_to_all | solution.py:122
  103.0 6.8 %reshape.190 = bf16[8,4,2,20,1536]{4,3,2,1,0:T(8,128)(2,1)} reshape(bf16[1280,1536]{1,0:T(8,128)(2,1)} %all-gather.9.cloned.1.call-done) | data formatting | bytes 7864320 | tf_op jit(solution)/shard_map/reshape | solution.py:65
  109.8 3.1 %slice_bitcast_fusion = (bf16[4,8,20,1536]{3,2,0,1:T(8,128)(2,1)S(1)}, bf16[4,8,20,1536]{3,2,0,1:T(8,128)(2,1)S(1)}) fusion(bf16[8,4,2,20,1536]{4,3,2,1,0:T(8,128)(2,1)} %reshape.190), kind=kLoop, calls=%fused_computation.20 | loop fusion | bytes 7864320 | tf_op jit(solution)/shard_map/transpose | solution.py:69
  114.0 1.6 copy.133
  115.6 4.0 %reshape.191 = bf16[640,1536]{1,0:T(8,128)(2,1)} reshape(bf16[4,8,20,1536]{3,2,1,0:T(8,128)(2,1)} %copy.133) | data formatting | bytes 3932160 | tf_op jit(solution)/shard_map/reshape | solution.py:68
  119.5 4.1 %constant_dynamic-slice_fusion.1 = (bf16[1,160,1536]{2,0,1:T(2,128)(2,1)S(1)}, bf16[1,160,1536]{2,0,1:T(2,128)(2,1)S(1)}, bf16[1,160,1536]{2,0,1:T(2,128)(2,1)S(1)}, bf16[1,160,1536]{2,0,1:T(2,128)(2,1)S(1)}) fusion(bf16[4,160,1536]{2,0,1:T(4,128)(2,1)S(1)} %bitcast.118, s32[]{:T(128)S(6)} %select_n.74, s32[]{:T(128)S(6)} %select_n.76, s32[]{:T(128)S(6)} %select_n.72, ...), kind=kLoop, calls=%fused_computation.137 | loop fusion | bytes 3932176 | tf_op jit(solution)/shard_map/jit(dynamic_index_in_dim)/dynamic_slice | solution.py:156
  124.3 1.5 convolution_add_fusion.2
  125.8 1.5 fusion.55
  127.4 2.7 %fusion.13 = bf16[512,1536]{1,0:T(8,128)(2,1)} fusion(f32[512,1536]{1,0:T(8,128)S(1)} %fusion.55, f32[512,1536]{1,0:T(8,128)S(1)} %convolution_add_fusion.2, bf16[160,512]{1,0:T(8,128)(2,1)} %collective-permute-done.4, bf16[1,160,1536]{2,0,1:T(2,128)(2,1)S(1)} %get-tuple-element.33), kind=kOutput, calls=%fused_computation.19 | convolution fusion | flops 254017536 | bytes 8519680 | tf_op jit(solution)/shard_map/dot_general | solution.py:154
  130.0 1.5 all-to-all-done
  131.5 2.1 %convert_reduce_fusion = f32[20,6144]{1,0:T(8,128)S(1)} fusion(bf16[8,20,6144]{2,1,0:T(8,128)(2,1)} %all-to-all-done), kind=kLoop, calls=%fused_computation.15 | loop fusion | flops 1843200 | bytes 2457600 | tf_op jit(solution)/shard_map/reduce_sum | solution.py:123
  134.2 8.4 %all-gather.3 = f32[49152]{0:T(1024)S(1)} all-gather(f32[6144]{0:T(1024)S(1)} %bitcast.120), channel_id=5, replica_groups=mesh['dp'=4,'ctx'=8] {'ctx'}, dimensions={0}, use_global_device_ids=true | all-gather | bytes 221184 | tf_op jit(solution)/shard_map/all_gather | solution.py:129
  144.9 2.8 %fusion.2 = bf16[1,128,6144]{2,1,0:T(8,128)(2,1)} fusion(bf16[1,128,6144]{2,1,0:T(8,128)(2,1)S(1)} %copy-done.4, f32[20,6144]{1,0:T(8,128)S(1)} %convert_reduce_fusion, f32[20]{0:T(128)S(1)} %fusion.44, s32[20]{0:T(128)S(1)} %bitcast.128, pred[20]{0:T(512)(128)(4,1)S(1)} %get-tuple-element.26), kind=kOutput, calls=%fused_computation.5 | convolution fusion | flops 191230976 | bytes 3637428 | tf_op jit(solution)/shard_map/dot_general | solution.py:125
  148.0 2.0 %collective-permute-done.6 = f32[6144]{0:T(1024)S(1)} collective-permute-done((f32[6144]{0:T(1024)S(1)}, f32[6144]{0:T(1024)S(1)}, u32[]{:S(2)}, u32[]{:S(2)}) %collective-permute-start.6) | collective-permute-done | bytes 24608 | tf_op jit(solution)/shard_map/ppermute | solution.py:165
  152.1 6.1 %convolution_convert_fusion = bf16[1536,1536]{1,0:T(8,128)(2,1)S(1)} fusion(bf16[640,1536]{1,0:T(8,128)(2,1)} %reshape.191, bf16[640,1536]{1,0:T(8,128)(2,1)} %all-gather.11.cloned.1.call-done), kind=kOutput, calls=%fused_computation.1 | convolution fusion | flops 3022258176 | bytes 8650752 | tf_op jit(solution)/shard_map/dot_general | solution.py:135
  158.2 2.3 %fusion.112 = (bf16[1536,512]{1,0:T(8,128)(2,1)}, bf16[1536,512]{1,0:T(8,128)(2,1)}, bf16[1536,512]{1,0:T(8,128)(2,1)}) fusion(bf16[1536,1536]{1,0:T(8,128)(2,1)S(1)} %convolution_convert_fusion), kind=kLoop, calls=%fused_computation.160 | loop fusion | bytes 9437184 | tf_op jit(solution)/shard_map/slice | solution.py:142
  (92 shorter events, 20.5 us)
Async XLA Ops:
  7.2 5.7 %copy-start = (bf16[1,128,6144]{2,1,0:T(8,128)(2,1)S(1)}, bf16[1,128,6144]{2,1,0:T(8,128)(2,1)}, u32[]{:S(2)}) copy-start(bf16[1,128,6144]{2,1,0:T(8,128)(2,1)} %param.12) | copy-start | bytes 4718596
  7.2 50.4 %all-gather.13.cloned.1.call-start = ((), (), s32[]{:S(2)}) async-start(), calls=%async_computation.3 | async-start | bytes 5363712 | tf_op jit(solution)/shard_map/all_gather | solution.py:47
  11.3 1.5 copy-start.2
  15.7 87.3 %all-gather.9.cloned.1.call-start = ((), (), s32[]{:S(2)}) async-start(), calls=%async_computation.1 | async-start | bytes 4423680 | tf_op jit(solution)/shard_map/all_gather | solution.py:65
  17.6 8.8 %collective-permute-start = (bf16[40,1536]{1,0:T(8,128)(2,1)S(1)}, bf16[40,1536]{1,0:T(8,128)(2,1)S(1)}, u32[]{:S(2)}, u32[]{:S(2)}) collective-permute-start(bf16[40,1536]{1,0:T(8,128)(2,1)S(1)} %get-tuple-element.39), channel_id=1, source_target_pairs={{0,24},{8,0},{16,8},{24,16},{1,25},{9,1},{17,9},{25,17},{2,26},{10... | collective-permute-start | bytes 368648 | tf_op jit(solution)/shard_map/ppermute | solution.py:62
  22.7 11.0 %collective-permute-start.2 = (bf16[40,1536]{1,0:T(8,128)(2,1)S(1)}, bf16[40,1536]{1,0:T(8,128)(2,1)S(1)}, u32[]{:S(2)}, u32[]{:S(2)}) collective-permute-start(bf16[40,1536]{1,0:T(8,128)(2,1)S(1)} %get-tuple-element.37), channel_id=1, source_target_pairs={{0,8},{8,16},{16,24},{24,0},{1,9},{9,17},{17,25},{25,1},{2,10},{10... | collective-permute-start | bytes 368648 | tf_op jit(solution)/shard_map/ppermute | solution.py:62
  22.7 10.9 %collective-permute-start.1 = (bf16[40,1536]{1,0:T(8,128)(2,1)S(1)}, bf16[40,1536]{1,0:T(8,128)(2,1)S(1)}, u32[]{:S(2)}, u32[]{:S(2)}) collective-permute-start(bf16[40,1536]{1,0:T(8,128)(2,1)S(1)} %get-tuple-element.38), channel_id=1, source_target_pairs={{0,16},{8,24},{16,0},{24,8},{1,17},{9,25},{17,1},{25,9},{2,18},{10... | collective-permute-start | bytes 368648 | tf_op jit(solution)/shard_map/ppermute | solution.py:62
  75.5 0.7 copy-start.6
  76.8 50.5 %collective-permute-start.4 = (bf16[160,512]{1,0:T(8,128)(2,1)}, bf16[160,512]{1,0:T(8,128)(2,1)}, u32[]{:S(2)}, u32[]{:S(2)}) collective-permute-start(bf16[160,512]{1,0:T(8,128)(2,1)} %bitcast.115), channel_id=1, source_target_pairs={{0,16},{8,24},{16,0},{24,8},{1,17},{9,25},{17,1},{25,9},{2,18},{10... | collective-permute-start | bytes 491528 | tf_op jit(solution)/shard_map/ppermute | solution.py:152
  79.2 45.1 %collective-permute-start.3 = (bf16[160,512]{1,0:T(8,128)(2,1)}, bf16[160,512]{1,0:T(8,128)(2,1)}, u32[]{:S(2)}, u32[]{:S(2)}) collective-permute-start(bf16[160,512]{1,0:T(8,128)(2,1)} %bitcast.115), channel_id=1, source_target_pairs={{0,8},{8,16},{16,24},{24,0},{1,9},{9,17},{17,25},{25,1},{2,10},{10... | collective-permute-start | bytes 491528 | tf_op jit(solution)/shard_map/ppermute | solution.py:152
  80.6 45.2 %collective-permute-start.5 = (bf16[160,512]{1,0:T(8,128)(2,1)}, bf16[160,512]{1,0:T(8,128)(2,1)}, u32[]{:S(2)}, u32[]{:S(2)}) collective-permute-start(bf16[160,512]{1,0:T(8,128)(2,1)} %bitcast.115), channel_id=1, source_target_pairs={{0,24},{8,0},{16,8},{24,16},{1,25},{9,1},{17,9},{25,17},{2,26},{10... | collective-permute-start | bytes 491528 | tf_op jit(solution)/shard_map/ppermute | solution.py:152
  97.7 33.8 %all-to-all-start = ((bf16[8,20,6144]{2,1,0:T(8,128)(2,1)}), bf16[8,20,6144]{2,1,0:T(8,128)(2,1)}, u32[]{:S(2)}, u32[]{:S(2)}) async-start(bf16[8,20,6144]{2,1,0:T(8,128)(2,1)} %convolution_convert_fusion.1), calls=%async_computation | async-start | bytes 4718592 | tf_op jit(solution)/shard_map/all_to_all | solution.py:122
  102.0 50.0 %all-gather.11.cloned.1.call-start = ((), (), s32[]{:S(2)}) async-start(), calls=%async_computation.2 | async-start | bytes 2457600 | tf_op jit(solution)/shard_map/all_gather | solution.py:130
  119.5 4.1 %copy-start.7 = (bf16[4,20,8,128]{3,2,1,0:T(8,128)(2,1)S(1)}, bf16[4,20,8,128]{3,2,1,0:T(8,128)(2,1)}, u32[]{:S(2)}) copy-start(bf16[4,20,8,128]{3,2,1,0:T(8,128)(2,1)} %copy-done.6) | copy-start | bytes 491524
  130.0 3.6 %copy-start.5 = (f32[20,6144]{1,0:T(8,128)S(1)}, f32[20,6144]{1,0:T(8,128)}, u32[]{:S(2)}) copy-start(f32[20,6144]{1,0:T(8,128)} %get-tuple-element.43) | copy-start | bytes 1474564
  130.0 3.8 %copy-start.3 = (f32[20,6144]{1,0:T(8,128)S(1)}, f32[20,6144]{1,0:T(8,128)}, u32[]{:S(2)}) copy-start(f32[20,6144]{1,0:T(8,128)} %copy-done.2) | copy-start | bytes 1474564
  130.0 14.8 %copy-start.4 = (bf16[1,128,6144]{2,1,0:T(8,128)(2,1)S(1)}, bf16[1,128,6144]{2,1,0:T(8,128)(2,1)}, u32[]{:S(2)}) copy-start(bf16[1,128,6144]{2,1,0:T(8,128)(2,1)} %param.11) | copy-start | bytes 4718596
  142.8 8.0 %collective-permute-start.8 = (f32[6144]{0:T(1024)S(1)}, f32[6144]{0:T(1024)S(1)}, u32[]{:S(2)}, u32[]{:S(2)}) collective-permute-start(f32[6144]{0:T(1024)S(1)} %reduce_sum.108), channel_id=1, source_target_pairs={{0,24},{8,0},{16,8},{24,16},{1,25},{9,1},{17,9},{25,17},{2,26},{10... | collective-permute-start | bytes 73736 | tf_op jit(solution)/shard_map/ppermute | solution.py:165
  143.5 6.9 %collective-permute-start.7 = (f32[6144]{0:T(1024)S(1)}, f32[6144]{0:T(1024)S(1)}, u32[]{:S(2)}, u32[]{:S(2)}) collective-permute-start(f32[6144]{0:T(1024)S(1)} %reduce_sum.108), channel_id=1, source_target_pairs={{0,16},{8,24},{16,0},{24,8},{1,17},{9,25},{17,1},{25,9},{2,18},{10... | collective-permute-start | bytes 73736 | tf_op jit(solution)/shard_map/ppermute | solution.py:165
  144.4 5.6 %collective-permute-start.6 = (f32[6144]{0:T(1024)S(1)}, f32[6144]{0:T(1024)S(1)}, u32[]{:S(2)}, u32[]{:S(2)}) collective-permute-start(f32[6144]{0:T(1024)S(1)} %reduce_sum.108), channel_id=1, source_target_pairs={{0,8},{8,16},{16,24},{24,0},{1,9},{9,17},{17,25},{25,1},{2,10},{10... | collective-permute-start | bytes 73736 | tf_op jit(solution)/shard_map/ppermute | solution.py:165
  152.1 8.4 %copy-start.1 = (bf16[1,128,6144]{2,1,0:T(8,128)(2,1)S(1)}, bf16[1,128,6144]{2,1,0:T(8,128)(2,1)}, u32[]{:S(2)}) copy-start(bf16[1,128,6144]{2,1,0:T(8,128)(2,1)} %param.12) | copy-start | bytes 4718596
Sparse Core Ops, SparseCore 0:
  15.8 41.8 all-gather.12
  60.1 35.6 all-gather.8
  104.5 42.7 all-gather.10
